TPU v7x, 256 devices: a whole 4x4x8 slice. The times are simulated.
256 devices in a mesh: req: 64 (over z, y_lo, x), tp: 4 (over y_hi, core).
Axes of the slice: x: 4, y: 4 (y_hi: 2, y_lo: 2; y = y_hi * 2 + y_lo), z: 8, core: 2. Of those that a mesh axis runs over, the one named last changes fastest.
Arguments:
- hidden: bfloat16 [32768, 4096], P(('req', 'tp')), may hold values from -6 to 6
- norm_gain: bfloat16 [4096], replicated, may hold values from 0.099609375 to 1.8984375
- w_qkv: bfloat16 [4096, 3072], P('req', 'tp'), may hold values from -0.09375 to 0.09375
- w_out: bfloat16 [2048, 4096], P('tp', 'req'), may hold values from -0.125 to 0.125
- lengths: int32 [256], replicated, may hold values from 1 to 3072, as said below
- deal: int32 [256], replicated, may hold values from 0 to 255, as said below
- pages: int32 [256, 24], P('req'), may hold values from 0 to 95, as said below
- pool: bfloat16 [6144, 128, 1024], P('req', None, 'tp'), may hold values from -360 to 360
Outputs:
- attn_out: bfloat16 [32768, 4096], P(('req', 'tp'))
- new_kv: bfloat16 [32768, 1024], P('req', 'tp')
Inputs may be any that keep to these rules, and one draw needn't show every extreme that they name: `lengths`: at least one request has exactly 3072 cached tokens. `deal`: a permutation of the requests. `pages`: the 4 rows of one req index together hold each page number of its pool block once.
All inputs are finite; a program needn't handle non-finite values.
Results may differ from a plain program's by a relative error of at most 0.01.
The roundings to bfloat16 on the way count: a program that leaves them out, or rounds other values in their place, can miss the bound.
Values may be sent and summed in bfloat16 or wider, within the bound.
No kernel may reach another device: no remote copies, remote signals or barrier semaphores. Data moves between devices by JAX's collectives and lax.ppermute only.
A program may use at most 128 MiB of HBM per device.

v0:
```python
import math
import jax
import jax.numpy as jnp
from jax import lax
from jax.sharding import PartitionSpec as P

HEAD = 128
QH = 16
KVH = 4
PAGE = 128
NEW = 128


def rotate(values, position):
    half = values.shape[-1] // 2
    freqs = 500000.0 ** (-(jnp.arange(half, dtype=jnp.float32) * 2.0 / values.shape[-1]))
    angles = position.astype(jnp.float32)[:, None] * freqs[None, :]
    target = (angles.shape[0],) + (1,) * (values.ndim - 2) + (half,)
    cosine = jnp.cos(angles).reshape(target)
    sine = jnp.sin(angles).reshape(target)
    former = values[..., :half]
    latter = values[..., half:]
    return jnp.concatenate([former * cosine - latter * sine, latter * cosine + former * sine], -1)


def fresh_scores_of(query_matrix, recent_key_rows, score_scale):
    scores = (
        jnp.einsum(
            "eksv,qkv->kseq", query_matrix, recent_key_rows, preferred_element_type=jnp.float32
        )
        * score_scale
    )
    count_new = query_matrix.shape[0]
    causal = jnp.arange(count_new)[:, None] >= jnp.arange(count_new)[None, :]
    return jnp.where(causal, scores, -jnp.inf)


def value_weighted_rows(weights, values, form):
    return jnp.einsum(
        form, weights.astype(jnp.bfloat16), values, preferred_element_type=jnp.float32
    )


def padded_attention(
    query_matrix, recent_key_rows, recent_value_rows, pool_view, page_row, length, score_scale
):
    heads_here = pool_view.shape[2]
    cache = pool_view[page_row].reshape(-1, heads_here, 2, HEAD)
    span = cache.shape[0]
    cached_scores = (
        jnp.einsum(
            "nhgd,khd->hgnk", query_matrix, cache[:, :, 0], preferred_element_type=jnp.float32
        )
        * score_scale
    )
    cached_scores = jnp.where(jnp.arange(span, dtype=jnp.int32) < length, cached_scores, -jnp.inf)
    recent_score_rows = fresh_scores_of(query_matrix, recent_key_rows, score_scale)
    row_max = jnp.maximum(cached_scores.max(-1), recent_score_rows.max(-1))[..., None]
    cached_exp = jnp.exp(cached_scores - row_max)
    recent_exponent = jnp.exp(recent_score_rows - row_max)
    total = cached_exp.sum(-1) + recent_exponent.sum(-1)
    summed_total = value_weighted_rows(cached_exp, cache[:, :, 1], "hgnk,khd->hgnd")
    summed_total = summed_total + value_weighted_rows(
        recent_exponent, recent_value_rows, "tvqa,ats->tvqs"
    )
    return summed_total / total[..., None]


def per_device(hidden, norm_gain, w_qkv, w_out, lengths, deal, pages, pool):
    states = hidden.astype(jnp.float32)
    mean_square = jnp.mean(states * states, axis=1, keepdims=True)
    normed = (states * lax.rsqrt(mean_square + 1e-05) * norm_gain.astype(jnp.float32)).astype(
        jnp.bfloat16
    )
    gathered = lax.all_gather(normed, "tp", axis=0, tiled=True)
    tok_rows = gathered.shape[0]
    projected = jnp.dot(
        gathered,
        lax.all_gather(w_qkv, "req", axis=0, tiled=True),
        preferred_element_type=jnp.float32,
    ).astype(jnp.bfloat16)
    full_out = lax.all_gather(w_out, "req", axis=1, tiled=True)
    group = QH // KVH
    heads_here = w_qkv.shape[1] // ((group + 2) * HEAD)
    slot_count = tok_rows // NEW
    slot_ids = lax.axis_index("req") * slot_count + jnp.arange(slot_count, dtype=jnp.int32)
    slot_length = lengths[deal[slot_ids]]
    position = jnp.repeat(slot_length, NEW) + jnp.tile(jnp.arange(NEW, dtype=jnp.int32), slot_count)
    projected = projected.reshape(tok_rows, heads_here, group + 2, HEAD)
    queries = rotate(projected[:, :, :group].astype(jnp.float32), position).astype(jnp.bfloat16)
    keys_new = rotate(projected[:, :, group].astype(jnp.float32), position).astype(jnp.bfloat16)
    values_new = projected[:, :, group + 1]
    new_kv = jnp.stack([keys_new, values_new], 2).reshape(tok_rows, heads_here * 2 * HEAD)
    pool_view = pool.reshape(pool.shape[0], PAGE, heads_here, 2, HEAD)
    score_scale = 1.0 / math.sqrt(HEAD)

    def attend(local_slot):
        begin = local_slot * NEW
        query_matrix = lax.dynamic_slice_in_dim(queries, begin, NEW, 0)
        recent_key_rows = lax.dynamic_slice_in_dim(keys_new, begin, NEW, 0)
        recent_value_rows = lax.dynamic_slice_in_dim(values_new, begin, NEW, 0)
        page_row = pages[local_slot]
        length = slot_length[local_slot]
        result = padded_attention(
            query_matrix,
            recent_key_rows,
            recent_value_rows,
            pool_view,
            page_row,
            length,
            score_scale,
        )
        result = result.astype(jnp.bfloat16)
        return result.transpose(2, 0, 1, 3).reshape(NEW, heads_here * group * HEAD)

    contexts = lax.map(attend, jnp.arange(slot_count, dtype=jnp.int32))
    context = contexts.reshape(tok_rows, heads_here * group * HEAD)
    attn_out = lax.psum_scatter(
        jnp.dot(context, full_out, preferred_element_type=jnp.float32).astype(jnp.bfloat16),
        "tp",
        scatter_dimension=0,
        tiled=True,
    )
    return (attn_out, new_kv)


def solution(mesh):
    in_specs = (
        P(("req", "tp"), None),
        P(),
        P("req", "tp"),
        P("tp", "req"),
        P(),
        P(),
        P("req", None),
        P("req", None, "tp"),
    )
    out_specs = (P(("req", "tp"), None), P("req", "tp"))
    return jax.shard_map(
        per_device, mesh=mesh, in_specs=in_specs, out_specs=out_specs, check_vma=False
    )
```

profile of v0, /device:TPU:1, one launch (start us, length us, event | category | flops | bytes accessed | tf_op | source)
XLA Modules:
  0.0 734.8 jit_solution(14359055821439632575)
XLA Ops:
  7.9 1.5 fusion.32
  9.5 2.5 fusion.34
  15.0 9.7 %reshape.408 = bf16[96,128,1,2,128]{4,3,2,1,0:T(2,128)(2,1)} reshape(bf16[96,128,256]{2,1,0:T(8,128)(2,1)} %param.17) | data formatting | bytes 12582912 | tf_op jit(solution)/shard_map/reshape | solution.py:94
  25.3 32.2 %all-gather.4.cloned.1.call-done = bf16[512,4096]{1,0:T(8,128)(2,1)} async-done(((bf16[128,4096]{1,0:T(8,128)(2,1)}), bf16[512,4096]{1,0:T(8,128)(2,1)}) %all-gather.4.cloned.1.call-update) | async-done | bytes 4194320 | tf_op jit(solution)/shard_map/all_gather | solution.py:75
  57.4 262.9 %all-gather.6.cloned.1.call-done = bf16[4096,768]{1,0:T(8,128)(2,1)} async-done(((bf16[64,768]{1,0:T(8,128)(2,1)}), bf16[4096,768]{1,0:T(8,128)(2,1)}) %all-gather.6.cloned.1.call-update) | async-done | bytes 6291472 | tf_op jit(solution)/shard_map/all_gather | solution.py:79
  320.4 7.5 %convolution_convert_fusion.1 = bf16[512,768]{1,0:T(8,128)(2,1)S(1)} fusion(bf16[512,4096]{1,0:T(8,128)(2,1)} %all-gather.4.cloned.1.call-done, bf16[4096,768]{1,0:T(8,128)(2,1)} %all-gather.6.cloned.1.call-done), kind=kOutput, calls=%fused_computation.53 | convolution fusion | flops 3221618688 | bytes 11272192 | tf_op jit(solution)/shard_map/dot_general | solution.py:77
  329.1 76.6 %while.10 = (s32[]{:T(128)}, bf16[4,128,512]{2,1,0:T(8,128)(2,1)S(1)}, s32[4]{0:T(128)S(1)}, s32[4]{0:T(128)S(1)}, s32[4,24]{1,0:T(4,128)}, /*index=5*/bf16[96,1...) while((s32[]{:T(128)}, ...), condition=%wide.region_6.7_spmd, body=%wide.region_1.6_spmd.sunk | while | flops 856837184 | bytes 29113984 | solution.py:116
  333.0 8.2 %gather_fusion = bf16[24,128,2,128]{3,2,1,0:T(2,128)(2,1)S(1)} fusion(bf16[96,128,2,128]{3,2,1,0:T(2,128)(2,1)} %bitcast.156, s32[1024]{0:T(1024)S(1)} %pad_clamp_fusion.4), kind=kCustom, calls=%fused_computation.clone.1 | custom fusion | bytes 3145824 | tf_op jit(solution)/shard_map/while/body/eval_jaxpr/gather | solution.py:48
  344.2 2.0 fusion.67
  346.2 1.7 fusion.66
  352.1 8.2 %gather_fusion = bf16[24,128,2,128]{3,2,1,0:T(2,128)(2,1)S(1)} fusion(bf16[96,128,2,128]{3,2,1,0:T(2,128)(2,1)} %bitcast.156, s32[1024]{0:T(1024)S(1)} %pad_clamp_fusion.4), kind=kCustom, calls=%fused_computation.clone.1 | custom fusion | bytes 3145824 | tf_op jit(solution)/shard_map/while/body/eval_jaxpr/gather | solution.py:48
  363.3 2.0 fusion.67
  365.3 1.7 fusion.66
  371.3 8.2 %gather_fusion = bf16[24,128,2,128]{3,2,1,0:T(2,128)(2,1)S(1)} fusion(bf16[96,128,2,128]{3,2,1,0:T(2,128)(2,1)} %bitcast.156, s32[1024]{0:T(1024)S(1)} %pad_clamp_fusion.4), kind=kCustom, calls=%fused_computation.clone.1 | custom fusion | bytes 3145824 | tf_op jit(solution)/shard_map/while/body/eval_jaxpr/gather | solution.py:48
  381.1 1.0 bitcast_reduce_fusion.2
  382.4 2.0 fusion.67
  384.4 1.7 fusion.66
  390.4 8.2 %gather_fusion = bf16[24,128,2,128]{3,2,1,0:T(2,128)(2,1)S(1)} fusion(bf16[96,128,2,128]{3,2,1,0:T(2,128)(2,1)} %bitcast.156, s32[1024]{0:T(1024)S(1)} %pad_clamp_fusion.4), kind=kCustom, calls=%fused_computation.clone.1 | custom fusion | bytes 3145824 | tf_op jit(solution)/shard_map/while/body/eval_jaxpr/gather | solution.py:48
  400.3 1.0 bitcast_reduce_fusion.2
  401.6 2.0 fusion.67
  403.6 1.7 fusion.66
  405.7 216.2 %all-gather.8.cloned.1.call-done = bf16[512,4096]{0,1:T(8,128)(2,1)} async-done(((bf16[512,64]{0,1:T(8,128)(2,1)}), bf16[512,4096]{0,1:T(8,128)(2,1)}) %all-gather.8.cloned.1.call-update) | async-done | bytes 4194320 | tf_op jit(solution)/shard_map/all_gather | solution.py:82
  621.9 6.5 convolution_convert_fusion
  629.3 98.9 %reduce-scatter.2.cloned.1.call-done = bf16[128,4096]{1,0:T(8,128)(2,1)} async-done(((bf16[512,4096]{1,0:T(8,128)(2,1)}), bf16[128,4096]{1,0:T(8,128)(2,1)}) %reduce-scatter.2.cloned.1.call-update) | async-done | bytes 1048592 | tf_op jit(solution)/shard_map/reduce_scatter | solution.py:118
  (92 shorter events, 22.5 us)
Async XLA Ops:
  7.2 6.4 copy-start
  7.2 7.1 copy-start.1
  7.2 50.2 %all-gather.4.cloned.1.call-start = ((), (), s32[]{:S(2)}) async-start(), calls=%async_computation.1 | async-start | bytes 5242880 | tf_op jit(solution)/shard_map/all_gather | solution.py:75
  12.0 308.3 %all-gather.6.cloned.1.call-start = ((), (), s32[]{:S(2)}) async-start(), calls=%async_computation.2 | async-start | bytes 6389760 | tf_op jit(solution)/shard_map/all_gather | solution.py:79
  12.8 609.2 %all-gather.8.cloned.1.call-start = ((), (), s32[]{:S(2)}) async-start(), calls=%async_computation.3 | async-start | bytes 4259840 | tf_op jit(solution)/shard_map/all_gather | solution.py:82
  13.5 714.7 %reduce-scatter.2.cloned.1.call-start = ((), (), s32[]{:S(2)}) async-start(), calls=%async_computation.4 | async-start | bytes 5242880 | tf_op jit(solution)/shard_map/reduce_scatter | solution.py:118
Sparse Core Ops, SparseCore 0:
  12.1 45.2 all-gather.3
  59.2 261.0 all-gather.5
  322.1 299.7 all-gather.7
  628.6 99.5 reduce-scatter.1
where the time goes:
time: 736 us; the launch traced here: 735 us
  waiting for transfers between devices  612 us (83%)
  local copies, waits for them, and re-layouts  51.7 us (7%)
  matrix products  26.6 us (4%)
  other arithmetic  20 us (3%)
  between operations  13.9 us (2%)
  loops' own time  10.8 us (1%)
    all_gather x1, waiting for transfers between devices, per_device(): lax.all_gather(w_qkv, 'req', axis=0, tiled=True)  263 us
    all_gather x1, waiting for transfers between devices, per_device(): full_out = lax.all_gather(w_out, 'req', axis=1, tiled=True)  216 us
    reduce_scatter x1, waiting for transfers between devices, per_device(): lax.psum_scatter(jnp.dot(context, full_out, preferred_element_type=jnp.fl...  98.9 us
    gather x8, local copies, waits for them, and re-layouts, padded_attention(): cache = pool_view[page_row].reshape(-1, heads_here, 2, HEAD)  34.3 us
    all_gather x1, waiting for transfers between devices, per_device(): gathered = lax.all_gather(normed, 'tp', axis=0, tiled=True)  32.2 us
  transfers between devices with their start and end apart: 4, of which 4 were waited for; matrix products, arithmetic and copies ran while one was open for 12% of the time, Pallas kernels for 0%

commit v1 on v0

--- a/solution.py
+++ b/solution.py
@@ -9,6 +9,9 @@
 KVH = 4
 PAGE = 128
 NEW = 128
+lift_surface = lambda local_x, k_dim: jnp.concatenate(
+    lax.all_to_all(jnp.stack([local_x for _ in range(lax.psum(1, "req"))]), "req", 0, 0), k_dim
+)
 
 
 def rotate(values, position):
@@ -79,7 +82,7 @@
         lax.all_gather(w_qkv, "req", axis=0, tiled=True),
         preferred_element_type=jnp.float32,
     ).astype(jnp.bfloat16)
-    full_out = lax.all_gather(w_out, "req", axis=1, tiled=True)
+    full_out = lift_surface(w_out, 1)
     group = QH // KVH
     heads_here = w_qkv.shape[1] // ((group + 2) * HEAD)
     slot_count = tok_rows // NEW

time: 736 us -> 553 us (0.75)
  waiting for transfers between devices: 612 us -> 413 us
  starting transfers between devices: 0.16 us -> 13.9 us
    all_gather x1 -> x0, waiting for transfers between devices: 216 us -> none  [per_device(): full_out = lax.all_gather(w_out, 'req', axis=1, tiled=True)]
    all_to_all x0 -> x1, starting transfers between devices: none -> 13.8 us  [lax.all_to_all(jnp.stack([local_x for _ in range(lax.psum(1, 'req'))]), '...]
    all_gather x1, waiting for transfers between devices: 32.2 us -> 45.7 us  [per_device(): gathered = lax.all_gather(normed, 'tp', axis=0, tiled=True)]
  transfers between devices with their start and end apart: 4 -> 4, of which waited for: 4 -> 3; matrix products, arithmetic and copies ran while one was open for 12% -> 16% of each run, Pallas kernels for 0% -> 0%
where the time goes in v1:
time: 553 us; the launch traced here: 552 us
  waiting for transfers between devices  413 us (75%)
  local copies, waits for them, and re-layouts  54.3 us (10%)
  matrix products  26.6 us (5%)
  other arithmetic  20 us (4%)
  starting transfers between devices  13.9 us (3%)
  between operations  13.9 us (3%)
  loops' own time  10.8 us (2%)
    all_gather x1, waiting for transfers between devices, per_device(): lax.all_gather(w_qkv, 'req', axis=0, tiled=True)  270 us
    reduce_scatter x1, waiting for transfers between devices, per_device(): lax.psum_scatter(jnp.dot(context, full_out, preferred_element_type=jnp.fl...  96.6 us
    all_gather x1, waiting for transfers between devices, per_device(): gathered = lax.all_gather(normed, 'tp', axis=0, tiled=True)  45.7 us
    gather x8, local copies, waits for them, and re-layouts, padded_attention(): cache = pool_view[page_row].reshape(-1, heads_here, 2, HEAD)  34.3 us
    all_to_all x1, starting transfers between devices, lax.all_to_all(jnp.stack([local_x for _ in range(lax.psum(1, 'req'))]), '...  13.8 us
  transfers between devices with their start and end apart: 4, of which 3 were waited for; matrix products, arithmetic and copies ran while one was open for 16% of the time, Pallas kernels for 0%

profile of v1, /device:TPU:1, one launch (start us, length us, event | category | flops | bytes accessed | tf_op | source)
XLA Modules:
  0.0 552.1 jit_solution(7508195321610588339)
XLA Ops:
  7.9 1.5 fusion.32
  9.5 2.5 fusion.34
  12.8 2.4 stack.4
  15.2 13.8 %all-to-all-start = ((bf16[64,512,64]{1,2,0:T(8,128)(2,1)}), bf16[64,512,64]{1,2,0:T(8,128)(2,1)}, u32[]{:S(2)}, u32[]{:S(2)}) async-start(bf16[64,512,64]{1,2,0:T(8,128)(2,1)} %stack.4), calls=%async_computation | async-start | bytes 8388608 | tf_op jit(solution)/shard_map/all_to_all | solution.py:13
  29.1 9.9 %reshape.416 = bf16[96,128,1,2,128]{4,3,2,1,0:T(2,128)(2,1)} reshape(bf16[96,128,256]{2,1,0:T(8,128)(2,1)} %param.17) | data formatting | bytes 12582912 | tf_op jit(solution)/shard_map/reshape | solution.py:97
  40.9 45.7 %all-gather.3.cloned.1.call-done = bf16[512,4096]{1,0:T(8,128)(2,1)} async-done(((bf16[128,4096]{1,0:T(8,128)(2,1)}), bf16[512,4096]{1,0:T(8,128)(2,1)}) %all-gather.3.cloned.1.call-update) | async-done | bytes 4194320 | tf_op jit(solution)/shard_map/all_gather | solution.py:78
  86.5 269.7 %all-gather.5.cloned.1.call-done = bf16[4096,768]{1,0:T(8,128)(2,1)} async-done(((bf16[64,768]{1,0:T(8,128)(2,1)}), bf16[4096,768]{1,0:T(8,128)(2,1)}) %all-gather.5.cloned.1.call-update) | async-done | bytes 6291472 | tf_op jit(solution)/shard_map/all_gather | solution.py:82
  356.2 7.5 %convolution_convert_fusion.1 = bf16[512,768]{1,0:T(8,128)(2,1)S(1)} fusion(bf16[512,4096]{1,0:T(8,128)(2,1)} %all-gather.3.cloned.1.call-done, bf16[4096,768]{1,0:T(8,128)(2,1)} %all-gather.5.cloned.1.call-done), kind=kOutput, calls=%fused_computation.53 | convolution fusion | flops 3221618688 | bytes 11272192 | tf_op jit(solution)/shard_map/dot_general | solution.py:80
  365.0 76.6 %while.10 = (s32[]{:T(128)}, bf16[4,128,512]{2,1,0:T(8,128)(2,1)S(1)}, s32[4]{0:T(128)S(1)}, s32[4]{0:T(128)S(1)}, s32[4,24]{1,0:T(4,128)}, /*index=5*/bf16[96,1...) while((s32[]{:T(128)}, ...), condition=%wide.region_6.7_spmd, body=%wide.region_1.6_spmd.sunk | while | flops 856837184 | bytes 29113984 | solution.py:119
  368.9 8.2 %gather_fusion = bf16[24,128,2,128]{3,2,1,0:T(2,128)(2,1)S(1)} fusion(bf16[96,128,2,128]{3,2,1,0:T(2,128)(2,1)} %bitcast.159, s32[1024]{0:T(1024)S(1)} %pad_clamp_fusion.4), kind=kCustom, calls=%fused_computation.clone.1 | custom fusion | bytes 3145824 | tf_op jit(solution)/shard_map/while/body/eval_jaxpr/gather | solution.py:51
  380.1 2.0 fusion.67
  382.1 1.7 fusion.66
  388.0 8.2 %gather_fusion = bf16[24,128,2,128]{3,2,1,0:T(2,128)(2,1)S(1)} fusion(bf16[96,128,2,128]{3,2,1,0:T(2,128)(2,1)} %bitcast.159, s32[1024]{0:T(1024)S(1)} %pad_clamp_fusion.4), kind=kCustom, calls=%fused_computation.clone.1 | custom fusion | bytes 3145824 | tf_op jit(solution)/shard_map/while/body/eval_jaxpr/gather | solution.py:51
  399.2 2.0 fusion.67
  401.2 1.7 fusion.66
  407.2 8.2 %gather_fusion = bf16[24,128,2,128]{3,2,1,0:T(2,128)(2,1)S(1)} fusion(bf16[96,128,2,128]{3,2,1,0:T(2,128)(2,1)} %bitcast.159, s32[1024]{0:T(1024)S(1)} %pad_clamp_fusion.4), kind=kCustom, calls=%fused_computation.clone.1 | custom fusion | bytes 3145824 | tf_op jit(solution)/shard_map/while/body/eval_jaxpr/gather | solution.py:51
  417.0 1.0 bitcast_reduce_fusion.2
  418.3 2.0 fusion.67
  420.3 1.7 fusion.66
  426.3 8.2 %gather_fusion = bf16[24,128,2,128]{3,2,1,0:T(2,128)(2,1)S(1)} fusion(bf16[96,128,2,128]{3,2,1,0:T(2,128)(2,1)} %bitcast.159, s32[1024]{0:T(1024)S(1)} %pad_clamp_fusion.4), kind=kCustom, calls=%fused_computation.clone.1 | custom fusion | bytes 3145824 | tf_op jit(solution)/shard_map/while/body/eval_jaxpr/gather | solution.py:51
  437.5 2.0 fusion.67
  439.5 1.7 fusion.66
  441.6 6.5 %convolution_convert_fusion = bf16[512,4096]{1,0:T(8,128)(2,1)} fusion(bf16[512,512]{1,0:T(8,128)(2,1)S(1)} %bitcast.166, bf16[512,4096]{0,1:T(8,128)(2,1)} %bitcast.34), kind=kOutput, calls=%fused_computation.47 | convolution fusion | flops 2149580800 | bytes 8912896 | tf_op jit(solution)/shard_map/dot_general | solution.py:122
  449.0 96.6 %reduce-scatter.2.cloned.1.call-done = bf16[128,4096]{1,0:T(8,128)(2,1)} async-done(((bf16[512,4096]{1,0:T(8,128)(2,1)}), bf16[128,4096]{1,0:T(8,128)(2,1)}) %reduce-scatter.2.cloned.1.call-update) | async-done | bytes 1048592 | tf_op jit(solution)/shard_map/reduce_scatter | solution.py:121
  (94 shorter events, 22.8 us)
Async XLA Ops:
  7.2 31.8 %copy-start = (s32[256]{0:T(256)S(1)}, s32[256]{0:T(256)}, u32[]{:S(2)}) copy-start(s32[256]{0:T(256)} %param.15) | copy-start | bytes 3076
  7.2 5.6 %copy-start.2 = (bf16[512,64]{0,1:T(8,128)(2,1)S(1)}, bf16[512,64]{0,1:T(8,128)(2,1)}, u32[]{:S(2)}) copy-start(bf16[512,64]{0,1:T(8,128)(2,1)} %param.13) | copy-start | bytes 196612
  7.2 79.3 %all-gather.3.cloned.1.call-start = ((), (), s32[]{:S(2)}) async-start(), calls=%async_computation.2 | async-start | bytes 5242880 | tf_op jit(solution)/shard_map/all_gather | solution.py:78
  12.0 344.2 %all-gather.5.cloned.1.call-start = ((), (), s32[]{:S(2)}) async-start(), calls=%async_computation.3 | async-start | bytes 6389760 | tf_op jit(solution)/shard_map/all_gather | solution.py:82
  15.2 426.3 %all-to-all-start = ((bf16[64,512,64]{1,2,0:T(8,128)(2,1)}), bf16[64,512,64]{1,2,0:T(8,128)(2,1)}, u32[]{:S(2)}, u32[]{:S(2)}) async-start(bf16[64,512,64]{1,2,0:T(8,128)(2,1)} %stack.4), calls=%async_computation | async-start | bytes 8388608 | tf_op jit(solution)/shard_map/all_to_all | solution.py:13
  29.0 516.6 %reduce-scatter.2.cloned.1.call-start = ((), (), s32[]{:S(2)}) async-start(), calls=%async_computation.4 | async-start | bytes 5242880 | tf_op jit(solution)/shard_map/reduce_scatter | solution.py:121
  29.0 10.6 %copy-start.1 = (s32[256]{0:T(256)S(1)}, s32[256]{0:T(256)}, u32[]{:S(2)}) copy-start(s32[256]{0:T(256)} %param.14) | copy-start | bytes 3076
Sparse Core Ops, SparseCore 0:
  12.1 74.3 all-gather.2
  88.3 267.8 all-gather.4
  448.2 97.2 reduce-scatter.1
